TPU v7x, 512 devices: a whole 4x8x8 slice. The times are simulated.
512 devices in a mesh: section: 4 (over z_hi, core), seq: 32 (over x, y), head: 4 (over z_lo).
Axes of the slice: x: 4, y: 8, z: 8 (z_hi: 2, z_lo: 4; z = z_hi * 4 + z_lo), core: 2. Of those that a mesh axis runs over, the one named last changes fastest.
Arguments:
- query_heads: bfloat16 [4, 6144, 3072], P('section', 'seq', 'head'), may hold values from -6 to 6
- key_heads: bfloat16 [4, 6144, 3072], P('section', 'seq', 'head'), may hold values from -6 to 6
- value_heads: bfloat16 [4, 6144, 3072], P('section', 'seq', 'head'), may hold values from -6 to 6
- stream: bfloat16 [4, 6144, 3072], P('section', 'seq', 'head'), may hold values from -1.5 to 1.5
- out_weight: bfloat16 [4, 3072, 3072], P('section', 'head', 'seq'), may hold values from -0.109375 to 0.109375
- gate_scale: float32 [4, 3072], P('section', 'head'), may hold values from 0.5 to 1.5
- windows: int32 [16, 27], replicated, may hold values from -1 to 15, as said below
Outputs:
- handed: bfloat16 [4, 6144, 3072], P('section', 'seq', 'head')
Inputs may be any that keep to these rules, and one draw needn't show every extreme that they name: `windows`: row t lists, in an order drawn for each row, tile t + dt for every dt in -1, 0, 1 with 0 <= t + dt < 16 and tile t + dt in the same clip as t, and -1 in all its other slots; clips are runs of whole consecutive temporal tiles.
All inputs are finite; a program needn't handle non-finite values.
Results may differ from a plain program's by a relative error of at most 0.012.
Values may be sent and summed in bfloat16 or wider, within the bound.
No kernel may reach another device: no remote copies, remote signals or barrier semaphores. Data moves between devices by JAX's collectives and lax.ppermute only.
A program may use at most 64 MiB of HBM per device.

v0:
```python
from functools import partial
import math
import jax
import jax.numpy as jnp
from jax import lax
from jax.sharding import PartitionSpec as P

HD = 128
SPATIAL = 1


def shifted(block, axis, distance):
    devices = range(lax.axis_size(axis))
    route = [(i - distance, i) for i in devices if i - distance in devices]
    return lax.ppermute(block, axis, route)


def from_behind(value, axis, steps):
    count = lax.axis_size(axis)
    pairs = [(source, (source + steps) % count) for source in range(count)]
    return lax.ppermute(value, axis, pairs)


def split_heads(slab, head_count):
    return slab.reshape(slab.shape[0], head_count, slab.shape[1] // head_count)


def tile_maxima(key_slab, head_count, spatial_count):
    parts = split_heads(key_slab, head_count).astype(jnp.float32)
    lengths = jnp.sqrt(jnp.sum(parts * parts, axis=2))
    return jnp.max(lengths.reshape(spatial_count, -1, head_count), axis=1)


def slab_keep(nearby, slab_tile, in_range, spatial_count, temporal_count):
    first = jnp.clip(slab_tile, 0, temporal_count - 1) * spatial_count
    return lax.dynamic_slice_in_dim(nearby, first, spatial_count, 1) & in_range


def attend(
    running,
    slab_entry,
    keep,
    query_parts,
    row_bound,
    head_count,
    spatial_count,
    tile_rows,
    score_scale,
):
    weighted, summed = running
    row_count = query_parts.shape[0]
    slab_keys = split_heads(slab_entry[0], head_count)
    slab_values = split_heads(slab_entry[1], head_count)
    scores = (
        jnp.einsum("qhd,khd->hqk", query_parts, slab_keys, preferred_element_type=jnp.float32)
        * score_scale
    )
    row_keep = jnp.broadcast_to(
        keep[:, None, :, None], (spatial_count, tile_rows, spatial_count, tile_rows)
    )
    row_keep = row_keep.reshape(row_count, row_count)
    weights = jnp.where(row_keep[None], jnp.exp(scores - row_bound.T[:, :, None]), 0.0)
    summed = summed + jnp.sum(weights, axis=2)
    weighted = weighted + jnp.einsum(
        "hqk,khd->qhd",
        weights.astype(jnp.bfloat16),
        slab_values,
        preferred_element_type=jnp.float32,
    )
    return (weighted, summed)


def on_device(query_heads, key_heads, value_heads, stream, out_weight, gate_scale, windows):
    queries = query_heads[0]
    own_keys = key_heads[0]
    own_values = value_heads[0]
    row_count, feature_count = queries.shape
    head_count = feature_count // HD
    spatial_count = SPATIAL
    tile_rows = row_count // spatial_count
    tile_count = windows.shape[0]
    temporal_count = tile_count // spatial_count
    score_scale = 1.0 / math.sqrt(HD)
    seq_count = lax.axis_size("seq")
    position = lax.axis_index("seq")
    temporal = position // 2
    allowed = jnp.any(
        windows[:, :, None] == jnp.arange(tile_count, dtype=jnp.int32)[None, None, :], axis=1
    )
    nearby = lax.dynamic_slice_in_dim(allowed, temporal * spatial_count, spatial_count, 0)
    always = jnp.array(True)
    slabs = [(own_keys, own_values, temporal, always)]
    reach = min(3, seq_count - 1)
    offsets = list(range(1, reach + 1)) + list(range(-reach, 0))
    for offset in offsets:
        moved_keys, moved_values = shifted((own_keys, own_values), "seq", offset)
        source = position - offset
        in_range = (source >= 0) & (source < seq_count)
        slabs.append((moved_keys, moved_values, source // 2, in_range))
    keeps = [
        slab_keep(nearby, slab_entry[2], slab_entry[3], spatial_count, temporal_count)
        for slab_entry in slabs
    ]
    bound_tiles = jnp.zeros((spatial_count, head_count), jnp.float32)
    for slab_entry, keep in zip(slabs, keeps):
        maxima = tile_maxima(slab_entry[0], head_count, spatial_count)
        candidate = jnp.where(keep[:, :, None], maxima[None, :, :], 0.0)
        bound_tiles = jnp.maximum(bound_tiles, jnp.max(candidate, axis=1))
    query_parts = split_heads(queries, head_count)
    query_float = query_parts.astype(jnp.float32)
    query_lengths = jnp.sqrt(jnp.sum(query_float * query_float, axis=2))
    row_bound = query_lengths * jnp.repeat(bound_tiles, tile_rows, axis=0) * score_scale
    running = (
        jnp.zeros((row_count, head_count, HD), jnp.float32),
        jnp.zeros((head_count, row_count), jnp.float32),
    )
    for slab_entry, keep in zip(slabs, keeps):
        step_fn = partial(
            attend,
            slab_entry=slab_entry,
            keep=keep,
            query_parts=query_parts,
            row_bound=row_bound,
            head_count=head_count,
            spatial_count=spatial_count,
            tile_rows=tile_rows,
            score_scale=score_scale,
        )
        running = step_fn(running)
    weighted, summed = running
    attended = (
        (weighted / summed.T[:, :, None]).astype(jnp.bfloat16).reshape(row_count, feature_count)
    )
    head_terms = jnp.dot(
        attended,
        lax.all_gather(out_weight[0], "seq", axis=1, tiled=True),
        preferred_element_type=jnp.float32,
    )
    mixed = lax.psum_scatter(
        head_terms.astype(jnp.bfloat16), "head", scatter_dimension=1, tiled=True
    ).astype(jnp.float32)
    updated = (stream[0].astype(jnp.float32) + gate_scale[0][None, :] * mixed).astype(jnp.bfloat16)
    handed = from_behind(updated, "section", 1)
    return handed[None]


def solution(mesh):
    in_specs = (
        P("section", "seq", "head"),
        P("section", "seq", "head"),
        P("section", "seq", "head"),
        P("section", "seq", "head"),
        P("section", "head", "seq"),
        P("section", "head"),
        P(),
    )
    out_specs = P("section", "seq", "head")
    return jax.shard_map(
        on_device, mesh=mesh, in_specs=in_specs, out_specs=out_specs, check_vma=False
    )
```

profile of v0, /device:TPU:2, one launch (start us, length us, event | category | flops | bytes accessed | tf_op | source)
XLA Modules:
  0.0 199.8 jit_solution(8086827323401507072)
XLA Ops:
  7.3 6.1 %collective-permute-start.4 = (bf16[192,768]{1,0:T(8,128)(2,1)}, bf16[192,768]{1,0:T(8,128)(2,1)S(1)}, u32[]{:S(2)}, u32[]{:S(2)}) collective-permute-start(bf16[192,768]{1,0:T(8,128)(2,1)} %bitcast.145), channel_id=1, source_target_pairs={{8,0},{12,4},{16,8},{20,12},{24,16},{28,20},{32,24},{36,28},{40,32... | collective-permute-start | bytes 884744 | tf_op jit(solution)/shard_map/ppermute | solution.py:15
  13.5 3.3 %collective-permute-start.5 = (bf16[192,768]{1,0:T(8,128)(2,1)}, bf16[192,768]{1,0:T(8,128)(2,1)S(1)}, u32[]{:S(2)}, u32[]{:S(2)}) collective-permute-start(bf16[192,768]{1,0:T(8,128)(2,1)} %bitcast.146), channel_id=1, source_target_pairs={{4,0},{8,4},{12,8},{16,12},{20,16},{24,20},{28,24},{32,28},{36,32}... | collective-permute-start | bytes 884744 | tf_op jit(solution)/shard_map/ppermute | solution.py:15
  16.7 1.9 collective-permute-start.2
  18.7 7.8 %collective-permute-start.3 = (bf16[192,768]{1,0:T(8,128)(2,1)}, bf16[192,768]{1,0:T(8,128)(2,1)}, u32[]{:S(2)}, u32[]{:S(2)}) collective-permute-start(bf16[192,768]{1,0:T(8,128)(2,1)} %bitcast.148), channel_id=1, source_target_pairs={{12,0},{16,4},{20,8},{24,12},{28,16},{32,20},{36,24},{40,28},{44,3... | collective-permute-start | bytes 884744 | tf_op jit(solution)/shard_map/ppermute | solution.py:15
  26.5 2.6 %collective-permute-start = (bf16[192,768]{1,0:T(8,128)(2,1)}, bf16[192,768]{1,0:T(8,128)(2,1)S(1)}, u32[]{:S(2)}, u32[]{:S(2)}) collective-permute-start(bf16[192,768]{1,0:T(8,128)(2,1)} %bitcast.149), channel_id=1, source_target_pairs={{0,4},{4,8},{8,12},{12,16},{16,20},{20,24},{24,28},{28,32},{32,36}... | collective-permute-start | bytes 884744 | tf_op jit(solution)/shard_map/ppermute | solution.py:15
  38.0 2.0 %collective-permute-start.1 = (bf16[192,768]{1,0:T(8,128)(2,1)S(1)}, bf16[192,768]{1,0:T(8,128)(2,1)}, u32[]{:S(2)}, u32[]{:S(2)}) collective-permute-start(bf16[192,768]{1,0:T(8,128)(2,1)S(1)} %bitcast.150), channel_id=1, source_target_pairs={{0,8},{4,12},{8,16},{12,20},{16,24},{20,28},{24,32},{28,36},{32,40... | collective-permute-start | bytes 884744 | tf_op jit(solution)/shard_map/ppermute | solution.py:15
  40.7 2.5 %collective-permute-start.6 = (bf16[192,768]{1,0:T(8,128)(2,1)S(1)}, bf16[192,768]{1,0:T(8,128)(2,1)}, u32[]{:S(2)}, u32[]{:S(2)}) collective-permute-start(bf16[192,768]{1,0:T(8,128)(2,1)S(1)} %bitcast.151), channel_id=1, source_target_pairs={{0,4},{4,8},{8,12},{12,16},{16,20},{20,24},{24,28},{28,32},{32,36}... | collective-permute-start | bytes 884744 | tf_op jit(solution)/shard_map/ppermute | solution.py:15
  43.8 6.9 %collective-permute-start.10 = (bf16[192,768]{1,0:T(8,128)(2,1)S(1)}, bf16[192,768]{1,0:T(8,128)(2,1)}, u32[]{:S(2)}, u32[]{:S(2)}) collective-permute-start(bf16[192,768]{1,0:T(8,128)(2,1)S(1)} %bitcast.152), channel_id=1, source_target_pairs={{8,0},{12,4},{16,8},{20,12},{24,16},{28,20},{32,24},{36,28},{40,32... | collective-permute-start | bytes 884744 | tf_op jit(solution)/shard_map/ppermute | solution.py:15
  51.7 4.7 %collective-permute-done.3 = bf16[192,768]{1,0:T(8,128)(2,1)} collective-permute-done((bf16[192,768]{1,0:T(8,128)(2,1)}, bf16[192,768]{1,0:T(8,128)(2,1)}, u32[]{:S(2)}, u32[]{:S(2)}) %collective-permute-start.3) | collective-permute-done | bytes 294944 | tf_op jit(solution)/shard_map/ppermute | solution.py:15
  56.4 7.9 %collective-permute-start.9 = (bf16[192,768]{1,0:T(8,128)(2,1)S(1)}, bf16[192,768]{1,0:T(8,128)(2,1)}, u32[]{:S(2)}, u32[]{:S(2)}) collective-permute-start(bf16[192,768]{1,0:T(8,128)(2,1)S(1)} %bitcast.153), channel_id=1, source_target_pairs={{12,0},{16,4},{20,8},{24,12},{28,16},{32,20},{36,24},{40,28},{44,3... | collective-permute-start | bytes 884744 | tf_op jit(solution)/shard_map/ppermute | solution.py:15
  65.9 2.2 %collective-permute-start.8 = (bf16[192,768]{1,0:T(8,128)(2,1)S(1)}, bf16[192,768]{1,0:T(8,128)(2,1)S(1)}, u32[]{:S(2)}, u32[]{:S(2)}) collective-permute-start(bf16[192,768]{1,0:T(8,128)(2,1)S(1)} %bitcast.154), channel_id=1, source_target_pairs={{0,12},{4,16},{8,20},{12,24},{16,28},{20,32},{24,36},{28,40},{32,4... | collective-permute-start | bytes 884744 | tf_op jit(solution)/shard_map/ppermute | solution.py:15
  68.9 5.1 %collective-permute-start.11 = (bf16[192,768]{1,0:T(8,128)(2,1)S(1)}, bf16[192,768]{1,0:T(8,128)(2,1)}, u32[]{:S(2)}, u32[]{:S(2)}) collective-permute-start(bf16[192,768]{1,0:T(8,128)(2,1)S(1)} %bitcast.155), channel_id=1, source_target_pairs={{4,0},{8,4},{12,8},{16,12},{20,16},{24,20},{28,24},{32,28},{36,32}... | collective-permute-start | bytes 884744 | tf_op jit(solution)/shard_map/ppermute | solution.py:15
  78.9 1.4 fusion.93
  80.9 2.6 %collective-permute-start.7 = (bf16[192,768]{1,0:T(8,128)(2,1)S(1)}, bf16[192,768]{1,0:T(8,128)(2,1)S(1)}, u32[]{:S(2)}, u32[]{:S(2)}) collective-permute-start(bf16[192,768]{1,0:T(8,128)(2,1)S(1)} %bitcast.156), channel_id=1, source_target_pairs={{0,8},{4,12},{8,16},{12,20},{16,24},{20,28},{24,32},{28,36},{32,40... | collective-permute-start | bytes 884744 | tf_op jit(solution)/shard_map/ppermute | solution.py:15
  84.9 3.7 %collective-permute-done.9 = bf16[192,768]{1,0:T(8,128)(2,1)} collective-permute-done((bf16[192,768]{1,0:T(8,128)(2,1)S(1)}, bf16[192,768]{1,0:T(8,128)(2,1)}, u32[]{:S(2)}, u32[]{:S(2)}) %collective-permute-start.9) | collective-permute-done | bytes 294944 | tf_op jit(solution)/shard_map/ppermute | solution.py:15
  90.0 1.4 fusion.95
  91.9 2.7 %collective-permute-done.8 = bf16[192,768]{1,0:T(8,128)(2,1)S(1)} collective-permute-done((bf16[192,768]{1,0:T(8,128)(2,1)S(1)}, bf16[192,768]{1,0:T(8,128)(2,1)S(1)}, u32[]{:S(2)}, u32[]{:S(2)}) %collective-permute-start.8) | collective-permute-done | bytes 294944 | tf_op jit(solution)/shard_map/ppermute | solution.py:15
  97.1 1.4 convolution_add_fusion.1
  98.4 2.4 %collective-permute-done.7 = bf16[192,768]{1,0:T(8,128)(2,1)S(1)} collective-permute-done((bf16[192,768]{1,0:T(8,128)(2,1)S(1)}, bf16[192,768]{1,0:T(8,128)(2,1)S(1)}, u32[]{:S(2)}, u32[]{:S(2)}) %collective-permute-start.7) | collective-permute-done | bytes 294944 | tf_op jit(solution)/shard_map/ppermute | solution.py:15
  101.3 31.5 %all-gather.3.cloned.1.call-done = bf16[1,768,3072]{1,2,0:T(8,128)(2,1)} async-done(((bf16[1,768,96]{1,2,0:T(8,128)(2,1)}), bf16[1,768,3072]{1,2,0:T(8,128)(2,1)}) %all-gather.3.cloned.1.call-update) | async-done | bytes 4718608 | tf_op jit(solution)/shard_map/all_gather | solution.py:136
  132.8 5.1 %fusion.2 = bf16[192,3072]{1,0:T(8,128)(2,1)} fusion(bf16[1,768,3072]{1,2,0:T(8,128)(2,1)} %all-gather.3.cloned.1.call-done, bf16[6,24,8,128]{3,2,1,0:T(8,128)(2,1)S(1)} %fusion.33), kind=kOutput, calls=%fused_computation.2 | convolution fusion | flops 906559488 | bytes 6193152 | tf_op jit(solution)/shard_map/dot_general | solution.py:134
  138.6 37.7 %reduce-scatter.2.cloned.1.call-done = bf16[192,768]{1,0:T(8,128)(2,1)} async-done(((bf16[192,3072]{1,0:T(8,128)(2,1)}), bf16[192,768]{1,0:T(8,128)(2,1)}) %reduce-scatter.2.cloned.1.call-update) | async-done | bytes 294928 | tf_op jit(solution)/shard_map/reduce_scatter | solution.py:139
  177.4 1.9 collective-permute-start.12
  179.3 13.0 %collective-permute-done.12 = bf16[192,768]{1,0:T(8,128)(2,1)S(1)} collective-permute-done((bf16[192,768]{1,0:T(8,128)(2,1)S(1)}, bf16[192,768]{1,0:T(8,128)(2,1)S(1)}, u32[]{:S(2)}, u32[]{:S(2)}) %collective-permute-start.12) | collective-permute-done | bytes 294944 | tf_op jit(solution)/shard_map/ppermute | solution.py:21
  (74 shorter events, 24.1 us)
Async XLA Ops:
  6.5 126.3 %all-gather.3.cloned.1.call-start = ((), (), s32[]{:S(2)}) async-start(), calls=%async_computation.2 | async-start | bytes 4866048 | tf_op jit(solution)/shard_map/all_gather | solution.py:136
  7.3 169.1 %reduce-scatter.2.cloned.1.call-start = ((), (), s32[]{:S(2)}) async-start(), calls=%async_computation.1 | async-start | bytes 1474560 | tf_op jit(solution)/shard_map/reduce_scatter | solution.py:139
  7.3 25.1 %copy-start.5 = (s32[16,27]{1,0:T(8,128)S(1)}, s32[16,27]{1,0:T(8,128)}, u32[]{:S(2)}) copy-start(s32[16,27]{1,0:T(8,128)} %param.13) | copy-start | bytes 5188
  7.3 30.7 %collective-permute-start.4 = (bf16[192,768]{1,0:T(8,128)(2,1)}, bf16[192,768]{1,0:T(8,128)(2,1)S(1)}, u32[]{:S(2)}, u32[]{:S(2)}) collective-permute-start(bf16[192,768]{1,0:T(8,128)(2,1)} %bitcast.145), channel_id=1, source_target_pairs={{8,0},{12,4},{16,8},{20,12},{24,16},{28,20},{32,24},{36,28},{40,32... | collective-permute-start | bytes 884744 | tf_op jit(solution)/shard_map/ppermute | solution.py:15
  13.5 27.2 %collective-permute-start.5 = (bf16[192,768]{1,0:T(8,128)(2,1)}, bf16[192,768]{1,0:T(8,128)(2,1)S(1)}, u32[]{:S(2)}, u32[]{:S(2)}) collective-permute-start(bf16[192,768]{1,0:T(8,128)(2,1)} %bitcast.146), channel_id=1, source_target_pairs={{4,0},{8,4},{12,8},{16,12},{20,16},{24,20},{28,24},{32,28},{36,32}... | collective-permute-start | bytes 884744 | tf_op jit(solution)/shard_map/ppermute | solution.py:15
  16.7 27.1 %collective-permute-start.2 = (bf16[192,768]{1,0:T(8,128)(2,1)}, bf16[192,768]{1,0:T(8,128)(2,1)S(1)}, u32[]{:S(2)}, u32[]{:S(2)}) collective-permute-start(bf16[192,768]{1,0:T(8,128)(2,1)} %bitcast.147), channel_id=1, source_target_pairs={{0,12},{4,16},{8,20},{12,24},{16,28},{20,32},{24,36},{28,40},{32,4... | collective-permute-start | bytes 884744 | tf_op jit(solution)/shard_map/ppermute | solution.py:15
  18.7 37.7 %collective-permute-start.3 = (bf16[192,768]{1,0:T(8,128)(2,1)}, bf16[192,768]{1,0:T(8,128)(2,1)}, u32[]{:S(2)}, u32[]{:S(2)}) collective-permute-start(bf16[192,768]{1,0:T(8,128)(2,1)} %bitcast.148), channel_id=1, source_target_pairs={{12,0},{16,4},{20,8},{24,12},{28,16},{32,20},{36,24},{40,28},{44,3... | collective-permute-start | bytes 884744 | tf_op jit(solution)/shard_map/ppermute | solution.py:15
  26.5 39.4 %collective-permute-start = (bf16[192,768]{1,0:T(8,128)(2,1)}, bf16[192,768]{1,0:T(8,128)(2,1)S(1)}, u32[]{:S(2)}, u32[]{:S(2)}) collective-permute-start(bf16[192,768]{1,0:T(8,128)(2,1)} %bitcast.149), channel_id=1, source_target_pairs={{0,4},{4,8},{8,12},{12,16},{16,20},{20,24},{24,28},{28,32},{32,36}... | collective-permute-start | bytes 884744 | tf_op jit(solution)/shard_map/ppermute | solution.py:15
  30.4 2.7 %copy-start.2 = (bf16[1,192,768]{2,1,0:T(8,128)(2,1)S(1)}, bf16[1,192,768]{2,1,0:T(8,128)(2,1)}, u32[]{:S(2)}) copy-start(bf16[1,192,768]{2,1,0:T(8,128)(2,1)} %param.9) | copy-start | bytes 884740
  31.8 6.2 %copy-start.1 = (bf16[1,192,768]{2,1,0:T(8,128)(2,1)S(1)}, bf16[1,192,768]{2,1,0:T(8,128)(2,1)}, u32[]{:S(2)}) copy-start(bf16[1,192,768]{2,1,0:T(8,128)(2,1)} %param.8) | copy-start | bytes 884740
  38.0 2.7 %copy-start.3 = (bf16[192,768]{1,0:T(8,128)(2,1)}, bf16[192,768]{1,0:T(8,128)(2,1)S(1)}, u32[]{:S(2)}) copy-start(bf16[192,768]{1,0:T(8,128)(2,1)S(1)} %collective-permute-done.4) | copy-start | bytes 884740
  38.0 30.9 %collective-permute-start.1 = (bf16[192,768]{1,0:T(8,128)(2,1)S(1)}, bf16[192,768]{1,0:T(8,128)(2,1)}, u32[]{:S(2)}, u32[]{:S(2)}) collective-permute-start(bf16[192,768]{1,0:T(8,128)(2,1)S(1)} %bitcast.150), channel_id=1, source_target_pairs={{0,8},{4,12},{8,16},{12,20},{16,24},{20,28},{24,32},{28,36},{32,40... | collective-permute-start | bytes 884744 | tf_op jit(solution)/shard_map/ppermute | solution.py:15
  40.7 56.4 %collective-permute-start.6 = (bf16[192,768]{1,0:T(8,128)(2,1)S(1)}, bf16[192,768]{1,0:T(8,128)(2,1)}, u32[]{:S(2)}, u32[]{:S(2)}) collective-permute-start(bf16[192,768]{1,0:T(8,128)(2,1)S(1)} %bitcast.151), channel_id=1, source_target_pairs={{0,4},{4,8},{8,12},{12,16},{16,20},{20,24},{24,28},{28,32},{32,36}... | collective-permute-start | bytes 884744 | tf_op jit(solution)/shard_map/ppermute | solution.py:15
  43.8 37.1 %collective-permute-start.10 = (bf16[192,768]{1,0:T(8,128)(2,1)S(1)}, bf16[192,768]{1,0:T(8,128)(2,1)}, u32[]{:S(2)}, u32[]{:S(2)}) collective-permute-start(bf16[192,768]{1,0:T(8,128)(2,1)S(1)} %bitcast.152), channel_id=1, source_target_pairs={{8,0},{12,4},{16,8},{20,12},{24,16},{28,20},{32,24},{36,28},{40,32... | collective-permute-start | bytes 884744 | tf_op jit(solution)/shard_map/ppermute | solution.py:15
  56.4 32.2 %collective-permute-start.9 = (bf16[192,768]{1,0:T(8,128)(2,1)S(1)}, bf16[192,768]{1,0:T(8,128)(2,1)}, u32[]{:S(2)}, u32[]{:S(2)}) collective-permute-start(bf16[192,768]{1,0:T(8,128)(2,1)S(1)} %bitcast.153), channel_id=1, source_target_pairs={{12,0},{16,4},{20,8},{24,12},{28,16},{32,20},{36,24},{40,28},{44,3... | collective-permute-start | bytes 884744 | tf_op jit(solution)/shard_map/ppermute | solution.py:15
  65.9 28.6 %collective-permute-start.8 = (bf16[192,768]{1,0:T(8,128)(2,1)S(1)}, bf16[192,768]{1,0:T(8,128)(2,1)S(1)}, u32[]{:S(2)}, u32[]{:S(2)}) collective-permute-start(bf16[192,768]{1,0:T(8,128)(2,1)S(1)} %bitcast.154), channel_id=1, source_target_pairs={{0,12},{4,16},{8,20},{12,24},{16,28},{20,32},{24,36},{28,40},{32,4... | collective-permute-start | bytes 884744 | tf_op jit(solution)/shard_map/ppermute | solution.py:15
  68.9 26.3 %collective-permute-start.11 = (bf16[192,768]{1,0:T(8,128)(2,1)S(1)}, bf16[192,768]{1,0:T(8,128)(2,1)}, u32[]{:S(2)}, u32[]{:S(2)}) collective-permute-start(bf16[192,768]{1,0:T(8,128)(2,1)S(1)} %bitcast.155), channel_id=1, source_target_pairs={{4,0},{8,4},{12,8},{16,12},{20,16},{24,20},{28,24},{32,28},{36,32}... | collective-permute-start | bytes 884744 | tf_op jit(solution)/shard_map/ppermute | solution.py:15
  76.9 1.2 copy-start.4
  80.9 20.0 %collective-permute-start.7 = (bf16[192,768]{1,0:T(8,128)(2,1)S(1)}, bf16[192,768]{1,0:T(8,128)(2,1)S(1)}, u32[]{:S(2)}, u32[]{:S(2)}) collective-permute-start(bf16[192,768]{1,0:T(8,128)(2,1)S(1)} %bitcast.156), channel_id=1, source_target_pairs={{0,8},{4,12},{8,16},{12,20},{16,24},{20,28},{24,32},{28,36},{32,40... | collective-permute-start | bytes 884744 | tf_op jit(solution)/shard_map/ppermute | solution.py:15
  137.9 0.7 copy-start.6
  137.9 38.4 %copy-start = (bf16[1,192,768]{2,1,0:T(8,128)(2,1)S(1)}, bf16[1,192,768]{2,1,0:T(8,128)(2,1)}, u32[]{:S(2)}) copy-start(bf16[1,192,768]{2,1,0:T(8,128)(2,1)} %param.10) | copy-start | bytes 884740
  177.4 14.9 %collective-permute-start.12 = (bf16[192,768]{1,0:T(8,128)(2,1)S(1)}, bf16[192,768]{1,0:T(8,128)(2,1)S(1)}, u32[]{:S(2)}, u32[]{:S(2)}) collective-permute-start(bf16[192,768]{1,0:T(8,128)(2,1)S(1)} %fusion.34), channel_id=1, source_target_pairs={{0,128},{128,256},{256,384},{384,0},{1,129},{129,257},{257,385},{3... | collective-permute-start | bytes 884744 | tf_op jit(solution)/shard_map/ppermute | solution.py:21
Sparse Core Ops, SparseCore 0:
  10.5 122.2 all-gather.2
  138.0 38.2 reduce-scatter.1
where the time goes:
time: 201 us; the launch traced here: 200 us
  waiting for transfers between devices  96.7 us (48%)
  starting transfers between devices  52.9 us (26%)
  matrix products  17.7 us (9%)
  between operations  17.7 us (9%)
  local copies, waits for them, and re-layouts  9.76 us (5%)
  other arithmetic  4.97 us (2%)
    ppermute x12, starting transfers between devices, shifted(): return lax.ppermute(block, axis, route)  51 us
    reduce_scatter x1, waiting for transfers between devices, on_device(): lax.psum_scatter(head_terms.astype(jnp.bfloat16), 'head', scatter_dimensi...  37.7 us
    all_gather x1, waiting for transfers between devices, on_device(): lax.all_gather(out_weight[0], 'seq', axis=1, tiled=True)  31.5 us
    ppermute x12, waiting for transfers between devices, shifted(): return lax.ppermute(block, axis, route)  13.8 us
    ppermute x1, waiting for transfers between devices, from_behind(): return lax.ppermute(value, axis, pairs)  13 us
    dot_general x7, matrix products, attend(): jnp.einsum('hqk,khd->qhd', weights.astype(jnp.bfloat16), slab_values, pre...  6.68 us
    dot_general x7, matrix products, attend(): jnp.einsum('qhd,khd->hqk', query_parts, slab_keys, preferred_element_type...  5.98 us
    dot_general x1, matrix products, on_device(): jnp.dot(attended, lax.all_gather(out_weight[0], 'seq', axis=1, tiled=True...  5.07 us
  transfers between devices with their start and end apart: 15, of which 8 were waited for; matrix products, arithmetic and copies ran while one was open for 12% of the time, Pallas kernels for 0%

commit v1 on v0

--- a/solution.py
+++ b/solution.py
@@ -1,3 +1,4 @@
+import functools
 from functools import partial
 import math
 import jax
@@ -7,6 +8,18 @@
 
 HD = 128
 SPATIAL = 1
+
+
+def link_the_routes_all(local_array, which_axis):
+    return jnp.concatenate(
+        lax.all_to_all(
+            jnp.stack([local_array for _ in range(lax.psum(1, which_axis))], 0), which_axis, 0, 0
+        ),
+        1,
+    )
+
+
+prepare_the_samples = functools.partial(link_the_routes_all, which_axis="seq")
 
 
 def shifted(block, axis, distance):
@@ -132,9 +145,7 @@
         (weighted / summed.T[:, :, None]).astype(jnp.bfloat16).reshape(row_count, feature_count)
     )
     head_terms = jnp.dot(
-        attended,
-        lax.all_gather(out_weight[0], "seq", axis=1, tiled=True),
-        preferred_element_type=jnp.float32,
+        attended, prepare_the_samples(out_weight[0]), preferred_element_type=jnp.float32
     )
     mixed = lax.psum_scatter(
         head_terms.astype(jnp.bfloat16), "head", scatter_dimension=1, tiled=True

time: 201 us -> 286 us (1.42)
  the two profiles are of different devices: /device:TPU:2 before, /device:TPU:6 now
where the time goes in v1:
time: 286 us; the launch traced here: 285 us
  waiting for transfers between devices  164 us (57%)
  starting transfers between devices  69.5 us (24%)
  matrix products  17.8 us (6%)
  between operations  17.7 us (6%)
  local copies, waits for them, and re-layouts  11.4 us (4%)
  other arithmetic  4.96 us (2%)
    ppermute x12, waiting for transfers between devices, shifted(): return lax.ppermute(block, axis, route)  108 us
    ppermute x12, starting transfers between devices, shifted(): return lax.ppermute(block, axis, route)  56.9 us
    reduce_scatter x1, waiting for transfers between devices, on_device(): lax.psum_scatter(head_terms.astype(jnp.bfloat16), 'head', scatter_dimensi...  42.4 us
    ppermute x1, waiting for transfers between devices, from_behind(): return lax.ppermute(value, axis, pairs)  13 us
    all_to_all x1, starting transfers between devices, link_the_routes_all(): lax.all_to_all(jnp.stack([local_array for _ in range(lax.psum(1, which_ax...  10.6 us
    dot_general x7, matrix products, attend(): jnp.einsum('hqk,khd->qhd', weights.astype(jnp.bfloat16), slab_values, pre...  6.71 us
    dot_general x7, matrix products, attend(): jnp.einsum('qhd,khd->hqk', query_parts, slab_keys, preferred_element_type...  5.99 us
  transfers between devices with their start and end apart: 15, of which 8 were waited for; matrix products, arithmetic and copies ran while one was open for 8% of the time, Pallas kernels for 0%

profile of v1, /device:TPU:6, one launch (start us, length us, event | category | flops | bytes accessed | tf_op | source)
XLA Modules:
  0.0 284.9 jit_solution(13911816502245838694)
XLA Ops:
  6.5 3.6 %stack.3 = bf16[32,768,96]{1,2,0:T(8,128)(2,1)} broadcast(bf16[768,96]{0,1:T(8,128)(2,1)} %bitcast.157), dimensions={1,2} | broadcast | bytes 4866048 | tf_op jit(solution)/shard_map/stack | solution.py:16
  10.2 10.6 %all-to-all-start = ((bf16[32,768,96]{1,2,0:T(8,128)(2,1)}), bf16[32,768,96]{1,2,0:T(8,128)(2,1)}, u32[]{:S(2)}, u32[]{:S(2)}) async-start(bf16[32,768,96]{1,2,0:T(8,128)(2,1)} %stack.3), calls=%async_computation | async-start | bytes 9437184 | tf_op jit(solution)/shard_map/all_to_all | solution.py:15
  20.8 4.9 %collective-permute-start.5 = (bf16[192,768]{1,0:T(8,128)(2,1)S(1)}, bf16[192,768]{1,0:T(8,128)(2,1)S(1)}, u32[]{:S(2)}, u32[]{:S(2)}) collective-permute-start(bf16[192,768]{1,0:T(8,128)(2,1)S(1)} %bitcast.145), channel_id=1, source_target_pairs={{4,0},{8,4},{12,8},{16,12},{20,16},{24,20},{28,24},{32,28},{36,32}... | collective-permute-start | bytes 884744 | tf_op jit(solution)/shard_map/ppermute | solution.py:28
  25.7 4.3 %collective-permute-start.4 = (bf16[192,768]{1,0:T(8,128)(2,1)S(1)}, bf16[192,768]{1,0:T(8,128)(2,1)}, u32[]{:S(2)}, u32[]{:S(2)}) collective-permute-start(bf16[192,768]{1,0:T(8,128)(2,1)S(1)} %bitcast.146), channel_id=1, source_target_pairs={{8,0},{12,4},{16,8},{20,12},{24,16},{28,20},{32,24},{36,28},{40,32... | collective-permute-start | bytes 884744 | tf_op jit(solution)/shard_map/ppermute | solution.py:28
  30.0 3.4 %collective-permute-start.3 = (bf16[192,768]{1,0:T(8,128)(2,1)S(1)}, bf16[192,768]{1,0:T(8,128)(2,1)S(1)}, u32[]{:S(2)}, u32[]{:S(2)}) collective-permute-start(bf16[192,768]{1,0:T(8,128)(2,1)S(1)} %bitcast.147), channel_id=1, source_target_pairs={{12,0},{16,4},{20,8},{24,12},{28,16},{32,20},{36,24},{40,28},{44,3... | collective-permute-start | bytes 884744 | tf_op jit(solution)/shard_map/ppermute | solution.py:28
  33.3 4.3 %collective-permute-start.2 = (bf16[192,768]{1,0:T(8,128)(2,1)S(1)}, bf16[192,768]{1,0:T(8,128)(2,1)S(1)}, u32[]{:S(2)}, u32[]{:S(2)}) collective-permute-start(bf16[192,768]{1,0:T(8,128)(2,1)S(1)} %bitcast.148), channel_id=1, source_target_pairs={{0,12},{4,16},{8,20},{12,24},{16,28},{20,32},{24,36},{28,40},{32,4... | collective-permute-start | bytes 884744 | tf_op jit(solution)/shard_map/ppermute | solution.py:28
  37.6 3.7 %collective-permute-start.1 = (bf16[192,768]{1,0:T(8,128)(2,1)S(1)}, bf16[192,768]{1,0:T(8,128)(2,1)S(1)}, u32[]{:S(2)}, u32[]{:S(2)}) collective-permute-start(bf16[192,768]{1,0:T(8,128)(2,1)S(1)} %bitcast.149), channel_id=1, source_target_pairs={{0,8},{4,12},{8,16},{12,20},{16,24},{20,28},{24,32},{28,36},{32,40... | collective-permute-start | bytes 884744 | tf_op jit(solution)/shard_map/ppermute | solution.py:28
  48.2 83.1 %collective-permute-done.5 = bf16[192,768]{1,0:T(8,128)(2,1)S(1)} collective-permute-done((bf16[192,768]{1,0:T(8,128)(2,1)S(1)}, bf16[192,768]{1,0:T(8,128)(2,1)S(1)}, u32[]{:S(2)}, u32[]{:S(2)}) %collective-permute-start.5) | collective-permute-done | bytes 294944 | tf_op jit(solution)/shard_map/ppermute | solution.py:28
  131.3 5.8 %collective-permute-start = (bf16[192,768]{1,0:T(8,128)(2,1)S(1)}, bf16[192,768]{1,0:T(8,128)(2,1)}, u32[]{:S(2)}, u32[]{:S(2)}) collective-permute-start(bf16[192,768]{1,0:T(8,128)(2,1)S(1)} %bitcast.150), channel_id=1, source_target_pairs={{0,4},{4,8},{8,12},{12,16},{16,20},{20,24},{24,28},{28,32},{32,36}... | collective-permute-start | bytes 884744 | tf_op jit(solution)/shard_map/ppermute | solution.py:28
  137.8 8.6 %collective-permute-done.4 = bf16[192,768]{1,0:T(8,128)(2,1)} collective-permute-done((bf16[192,768]{1,0:T(8,128)(2,1)S(1)}, bf16[192,768]{1,0:T(8,128)(2,1)}, u32[]{:S(2)}, u32[]{:S(2)}) %collective-permute-start.4) | collective-permute-done | bytes 294944 | tf_op jit(solution)/shard_map/ppermute | solution.py:28
  146.4 10.8 %collective-permute-start.11 = (bf16[192,768]{1,0:T(8,128)(2,1)S(1)}, bf16[192,768]{1,0:T(8,128)(2,1)}, u32[]{:S(2)}, u32[]{:S(2)}) collective-permute-start(bf16[192,768]{1,0:T(8,128)(2,1)S(1)} %bitcast.151), channel_id=1, source_target_pairs={{4,0},{8,4},{12,8},{16,12},{20,16},{24,20},{28,24},{32,28},{36,32}... | collective-permute-start | bytes 884744 | tf_op jit(solution)/shard_map/ppermute | solution.py:28
  158.8 6.0 %collective-permute-done.3 = bf16[192,768]{1,0:T(8,128)(2,1)S(1)} collective-permute-done((bf16[192,768]{1,0:T(8,128)(2,1)S(1)}, bf16[192,768]{1,0:T(8,128)(2,1)S(1)}, u32[]{:S(2)}, u32[]{:S(2)}) %collective-permute-start.3) | collective-permute-done | bytes 294944 | tf_op jit(solution)/shard_map/ppermute | solution.py:28
  164.8 3.0 %collective-permute-start.10 = (bf16[192,768]{1,0:T(8,128)(2,1)S(1)}, bf16[192,768]{1,0:T(8,128)(2,1)}, u32[]{:S(2)}, u32[]{:S(2)}) collective-permute-start(bf16[192,768]{1,0:T(8,128)(2,1)S(1)} %bitcast.152), channel_id=1, source_target_pairs={{8,0},{12,4},{16,8},{20,12},{24,16},{28,20},{32,24},{36,28},{40,32... | collective-permute-start | bytes 884744 | tf_op jit(solution)/shard_map/ppermute | solution.py:28
  168.7 6.5 %collective-permute-start.9 = (bf16[192,768]{1,0:T(8,128)(2,1)S(1)}, bf16[192,768]{1,0:T(8,128)(2,1)}, u32[]{:S(2)}, u32[]{:S(2)}) collective-permute-start(bf16[192,768]{1,0:T(8,128)(2,1)S(1)} %bitcast.153), channel_id=1, source_target_pairs={{12,0},{16,4},{20,8},{24,12},{28,16},{32,20},{36,24},{40,28},{44,3... | collective-permute-start | bytes 884744 | tf_op jit(solution)/shard_map/ppermute | solution.py:28
  176.0 1.9 collective-permute-start.8
  178.6 1.9 collective-permute-start.6
  185.5 1.4 fusion.87
  187.5 6.5 %collective-permute-start.7 = (bf16[192,768]{1,0:T(8,128)(2,1)S(1)}, bf16[192,768]{1,0:T(8,128)(2,1)S(1)}, u32[]{:S(2)}, u32[]{:S(2)}) collective-permute-start(bf16[192,768]{1,0:T(8,128)(2,1)S(1)} %bitcast.156), channel_id=1, source_target_pairs={{0,8},{4,12},{8,16},{12,20},{16,24},{20,28},{24,32},{28,36},{32,40... | collective-permute-start | bytes 884744 | tf_op jit(solution)/shard_map/ppermute | solution.py:28
  198.6 3.6 %collective-permute-done.9 = bf16[192,768]{1,0:T(8,128)(2,1)} collective-permute-done((bf16[192,768]{1,0:T(8,128)(2,1)S(1)}, bf16[192,768]{1,0:T(8,128)(2,1)}, u32[]{:S(2)}, u32[]{:S(2)}) %collective-permute-start.9) | collective-permute-done | bytes 294944 | tf_op jit(solution)/shard_map/ppermute | solution.py:28
  205.4 5.8 %collective-permute-done.6 = bf16[192,768]{1,0:T(8,128)(2,1)S(1)} collective-permute-done((bf16[192,768]{1,0:T(8,128)(2,1)S(1)}, bf16[192,768]{1,0:T(8,128)(2,1)S(1)}, u32[]{:S(2)}, u32[]{:S(2)}) %collective-permute-start.6) | collective-permute-done | bytes 294944 | tf_op jit(solution)/shard_map/ppermute | solution.py:28
  213.2 5.1 %convolution_convert_fusion = bf16[192,3072]{1,0:T(8,128)(2,1)} fusion(bf16[768,3072]{0,1:T(8,128)(2,1)} %bitcast.21, bf16[6,24,8,128]{3,2,1,0:T(8,128)(2,1)S(1)} %fusion.28), kind=kOutput, calls=%fused_computation | convolution fusion | flops 906559488 | bytes 6193152 | tf_op jit(solution)/shard_map/dot_general | solution.py:147
  218.9 42.4 %reduce-scatter.2.cloned.1.call-done = bf16[192,768]{1,0:T(8,128)(2,1)} async-done(((bf16[192,3072]{1,0:T(8,128)(2,1)}), bf16[192,768]{1,0:T(8,128)(2,1)}) %reduce-scatter.2.cloned.1.call-update) | async-done | bytes 294928 | tf_op jit(solution)/shard_map/reduce_scatter | solution.py:150
  262.4 1.9 collective-permute-start.12
  264.3 13.0 %collective-permute-done.12 = bf16[192,768]{1,0:T(8,128)(2,1)S(1)} collective-permute-done((bf16[192,768]{1,0:T(8,128)(2,1)S(1)}, bf16[192,768]{1,0:T(8,128)(2,1)S(1)}, u32[]{:S(2)}, u32[]{:S(2)}) %collective-permute-start.12) | collective-permute-done | bytes 294944 | tf_op jit(solution)/shard_map/ppermute | solution.py:34
  (76 shorter events, 25.1 us)
Async XLA Ops:
  10.1 10.6 %copy-start.2 = (bf16[1,192,768]{2,1,0:T(8,128)(2,1)S(1)}, bf16[1,192,768]{2,1,0:T(8,128)(2,1)}, u32[]{:S(2)}) copy-start(bf16[1,192,768]{2,1,0:T(8,128)(2,1)} %param.8) | copy-start | bytes 884740
  10.2 31.5 %copy-start.1 = (bf16[1,192,768]{2,1,0:T(8,128)(2,1)S(1)}, bf16[1,192,768]{2,1,0:T(8,128)(2,1)}, u32[]{:S(2)}) copy-start(bf16[1,192,768]{2,1,0:T(8,128)(2,1)} %param.7) | copy-start | bytes 884740
  10.2 203.0 %all-to-all-start = ((bf16[32,768,96]{1,2,0:T(8,128)(2,1)}), bf16[32,768,96]{1,2,0:T(8,128)(2,1)}, u32[]{:S(2)}, u32[]{:S(2)}) async-start(bf16[32,768,96]{1,2,0:T(8,128)(2,1)} %stack.3), calls=%async_computation | async-start | bytes 9437184 | tf_op jit(solution)/shard_map/all_to_all | solution.py:15
  20.7 240.6 %reduce-scatter.2.cloned.1.call-start = ((), (), s32[]{:S(2)}) async-start(), calls=%async_computation.2 | async-start | bytes 1474560 | tf_op jit(solution)/shard_map/reduce_scatter | solution.py:150
  20.8 21.8 %copy-start.6 = (s32[16,27]{1,0:T(8,128)S(1)}, s32[16,27]{1,0:T(8,128)}, u32[]{:S(2)}) copy-start(s32[16,27]{1,0:T(8,128)} %param.13) | copy-start | bytes 5188
  20.8 110.5 %collective-permute-start.5 = (bf16[192,768]{1,0:T(8,128)(2,1)S(1)}, bf16[192,768]{1,0:T(8,128)(2,1)S(1)}, u32[]{:S(2)}, u32[]{:S(2)}) collective-permute-start(bf16[192,768]{1,0:T(8,128)(2,1)S(1)} %bitcast.145), channel_id=1, source_target_pairs={{4,0},{8,4},{12,8},{16,12},{20,16},{24,20},{28,24},{32,28},{36,32}... | collective-permute-start | bytes 884744 | tf_op jit(solution)/shard_map/ppermute | solution.py:28
  25.7 120.7 %collective-permute-start.4 = (bf16[192,768]{1,0:T(8,128)(2,1)S(1)}, bf16[192,768]{1,0:T(8,128)(2,1)}, u32[]{:S(2)}, u32[]{:S(2)}) collective-permute-start(bf16[192,768]{1,0:T(8,128)(2,1)S(1)} %bitcast.146), channel_id=1, source_target_pairs={{8,0},{12,4},{16,8},{20,12},{24,16},{28,20},{32,24},{36,28},{40,32... | collective-permute-start | bytes 884744 | tf_op jit(solution)/shard_map/ppermute | solution.py:28
  30.0 134.9 %collective-permute-start.3 = (bf16[192,768]{1,0:T(8,128)(2,1)S(1)}, bf16[192,768]{1,0:T(8,128)(2,1)S(1)}, u32[]{:S(2)}, u32[]{:S(2)}) collective-permute-start(bf16[192,768]{1,0:T(8,128)(2,1)S(1)} %bitcast.147), channel_id=1, source_target_pairs={{12,0},{16,4},{20,8},{24,12},{28,16},{32,20},{36,24},{40,28},{44,3... | collective-permute-start | bytes 884744 | tf_op jit(solution)/shard_map/ppermute | solution.py:28
  33.3 135.4 %collective-permute-start.2 = (bf16[192,768]{1,0:T(8,128)(2,1)S(1)}, bf16[192,768]{1,0:T(8,128)(2,1)S(1)}, u32[]{:S(2)}, u32[]{:S(2)}) collective-permute-start(bf16[192,768]{1,0:T(8,128)(2,1)S(1)} %bitcast.148), channel_id=1, source_target_pairs={{0,12},{4,16},{8,20},{12,24},{16,28},{20,32},{24,36},{28,40},{32,4... | collective-permute-start | bytes 884744 | tf_op jit(solution)/shard_map/ppermute | solution.py:28
  37.6 138.3 %collective-permute-start.1 = (bf16[192,768]{1,0:T(8,128)(2,1)S(1)}, bf16[192,768]{1,0:T(8,128)(2,1)S(1)}, u32[]{:S(2)}, u32[]{:S(2)}) collective-permute-start(bf16[192,768]{1,0:T(8,128)(2,1)S(1)} %bitcast.149), channel_id=1, source_target_pairs={{0,8},{4,12},{8,16},{12,20},{16,24},{20,28},{24,32},{28,36},{32,40... | collective-permute-start | bytes 884744 | tf_op jit(solution)/shard_map/ppermute | solution.py:28
  41.7 1.7 copy-start.3
  131.3 15.1 %copy-start.4 = (bf16[192,768]{1,0:T(8,128)(2,1)}, bf16[192,768]{1,0:T(8,128)(2,1)S(1)}, u32[]{:S(2)}) copy-start(bf16[192,768]{1,0:T(8,128)(2,1)S(1)} %collective-permute-done.5) | copy-start | bytes 884740
  131.3 47.3 %collective-permute-start = (bf16[192,768]{1,0:T(8,128)(2,1)S(1)}, bf16[192,768]{1,0:T(8,128)(2,1)}, u32[]{:S(2)}, u32[]{:S(2)}) collective-permute-start(bf16[192,768]{1,0:T(8,128)(2,1)S(1)} %bitcast.150), channel_id=1, source_target_pairs={{0,4},{4,8},{8,12},{12,16},{16,20},{20,24},{24,28},{28,32},{32,36}... | collective-permute-start | bytes 884744 | tf_op jit(solution)/shard_map/ppermute | solution.py:28
  146.4 41.0 %collective-permute-start.11 = (bf16[192,768]{1,0:T(8,128)(2,1)S(1)}, bf16[192,768]{1,0:T(8,128)(2,1)}, u32[]{:S(2)}, u32[]{:S(2)}) collective-permute-start(bf16[192,768]{1,0:T(8,128)(2,1)S(1)} %bitcast.151), channel_id=1, source_target_pairs={{4,0},{8,4},{12,8},{16,12},{20,16},{24,20},{28,24},{32,28},{36,32}... | collective-permute-start | bytes 884744 | tf_op jit(solution)/shard_map/ppermute | solution.py:28
  164.8 30.5 %collective-permute-start.10 = (bf16[192,768]{1,0:T(8,128)(2,1)S(1)}, bf16[192,768]{1,0:T(8,128)(2,1)}, u32[]{:S(2)}, u32[]{:S(2)}) collective-permute-start(bf16[192,768]{1,0:T(8,128)(2,1)S(1)} %bitcast.152), channel_id=1, source_target_pairs={{8,0},{12,4},{16,8},{20,12},{24,16},{28,20},{32,24},{36,28},{40,32... | collective-permute-start | bytes 884744 | tf_op jit(solution)/shard_map/ppermute | solution.py:28
  168.7 33.4 %collective-permute-start.9 = (bf16[192,768]{1,0:T(8,128)(2,1)S(1)}, bf16[192,768]{1,0:T(8,128)(2,1)}, u32[]{:S(2)}, u32[]{:S(2)}) collective-permute-start(bf16[192,768]{1,0:T(8,128)(2,1)S(1)} %bitcast.153), channel_id=1, source_target_pairs={{12,0},{16,4},{20,8},{24,12},{28,16},{32,20},{36,24},{40,28},{44,3... | collective-permute-start | bytes 884744 | tf_op jit(solution)/shard_map/ppermute | solution.py:28
  176.0 27.5 %collective-permute-start.8 = (bf16[192,768]{1,0:T(8,128)(2,1)S(1)}, bf16[192,768]{1,0:T(8,128)(2,1)}, u32[]{:S(2)}, u32[]{:S(2)}) collective-permute-start(bf16[192,768]{1,0:T(8,128)(2,1)S(1)} %bitcast.154), channel_id=1, source_target_pairs={{0,12},{4,16},{8,20},{12,24},{16,28},{20,32},{24,36},{28,40},{32,4... | collective-permute-start | bytes 884744 | tf_op jit(solution)/shard_map/ppermute | solution.py:28
  178.6 32.6 %collective-permute-start.6 = (bf16[192,768]{1,0:T(8,128)(2,1)S(1)}, bf16[192,768]{1,0:T(8,128)(2,1)S(1)}, u32[]{:S(2)}, u32[]{:S(2)}) collective-permute-start(bf16[192,768]{1,0:T(8,128)(2,1)S(1)} %bitcast.155), channel_id=1, source_target_pairs={{0,4},{4,8},{8,12},{12,16},{16,20},{20,24},{24,28},{28,32},{32,36}... | collective-permute-start | bytes 884744 | tf_op jit(solution)/shard_map/ppermute | solution.py:28
  183.4 1.2 copy-start.5
  187.5 25.2 %collective-permute-start.7 = (bf16[192,768]{1,0:T(8,128)(2,1)S(1)}, bf16[192,768]{1,0:T(8,128)(2,1)S(1)}, u32[]{:S(2)}, u32[]{:S(2)}) collective-permute-start(bf16[192,768]{1,0:T(8,128)(2,1)S(1)} %bitcast.156), channel_id=1, source_target_pairs={{0,8},{4,12},{8,16},{12,20},{16,24},{20,28},{24,32},{28,36},{32,40... | collective-permute-start | bytes 884744 | tf_op jit(solution)/shard_map/ppermute | solution.py:28
  218.2 0.7 copy-start.7
  218.2 43.1 %copy-start = (bf16[1,192,768]{2,1,0:T(8,128)(2,1)S(1)}, bf16[1,192,768]{2,1,0:T(8,128)(2,1)}, u32[]{:S(2)}) copy-start(bf16[1,192,768]{2,1,0:T(8,128)(2,1)} %param.10) | copy-start | bytes 884740
  262.4 14.9 %collective-permute-start.12 = (bf16[192,768]{1,0:T(8,128)(2,1)S(1)}, bf16[192,768]{1,0:T(8,128)(2,1)S(1)}, u32[]{:S(2)}, u32[]{:S(2)}) collective-permute-start(bf16[192,768]{1,0:T(8,128)(2,1)S(1)} %fusion.29), channel_id=1, source_target_pairs={{0,128},{128,256},{256,384},{384,0},{1,129},{129,257},{257,385},{3... | collective-permute-start | bytes 884744 | tf_op jit(solution)/shard_map/ppermute | solution.py:34
Sparse Core Ops, SparseCore 0:
  218.4 42.9 reduce-scatter.1
